TPU v7x, 512 devices: a whole 4x8x8 slice. The times are simulated.
512 devices in a mesh: pb: 32 (over y, x), ka: 16 (over z, core).
Axes of the slice: x: 4, y: 8, z: 8, core: 2. Of those that a mesh axis runs over, the one named last changes fastest.
Arguments:
- queries: bfloat16 [65536, 1536], P(('pb', 'ka')), may hold values from -6 to 6
- keys: bfloat16 [65536, 1536], P(('pb', 'ka')), may hold values from -6 to 6
- values: bfloat16 [65536, 1536], P(('pb', 'ka')), may hold values from -6 to 6
- adjacency: int32 [512, 24], P(('pb', 'ka')), may hold values from -1 to 511, as said below
- counts: int32 [512], P(('pb', 'ka')), may hold values from 1 to 24, as said below
Outputs:
- attended: bfloat16 [65536, 1536], P(('pb', 'ka'))
Inputs may be any that keep to these rules, and one draw needn't show every extreme that they name: adjacency[i, 0] = i; entries 1 to counts[i] - 1 are distinct blocks from i - 31 to i - 1; the other entries are -1. counts[i] is at most min(i + 1, 32); the last block lists exactly 24.
All inputs are finite; a program needn't handle non-finite values.
Results may differ from a plain program's by a relative error of at most 0.0053.
Values may be sent and summed in bfloat16 or wider, within the bound.
No kernel may reach another device: no remote copies, remote signals or barrier semaphores. Data moves between devices by JAX's collectives and lax.ppermute only.
A program may use at most 128 MiB of HBM per device.

v0:
```python
import math
import jax
import jax.numpy as jnp
from jax import lax
from jax.sharding import PartitionSpec as P

DH = 128
NEG_FILL = -1e30


def passed_along(block, axis, distance):
    devices = range(lax.axis_size(axis))
    route = [(i - distance, i) for i in devices if i - distance in devices]
    return lax.ppermute(block, axis, route)


def tile_partials(query_rows, permitted, position, anchors, kv_window, current):
    sources, item_count, feature_width = query_rows.shape
    span_count = kv_window.shape[1]
    block_len = kv_window.shape[2]
    head_count = feature_width // DH
    grouped = math.gcd(sources, max(1, 512 // item_count))
    head_step = math.gcd(head_count, 4)
    scaling = 1.0 / math.sqrt(DH)
    key_window = kv_window[0].reshape(span_count, block_len, head_count, DH)
    value_window = kv_window[1].reshape(span_count, block_len, head_count, DH)
    leading = jnp.arange(span_count) == 0
    key_pos = jnp.arange(block_len, dtype=jnp.int32)

    def one_group(pieces):
        q_group, allow_group, pos_group, anchor_group = pieces
        q_group = q_group.reshape(grouped, item_count, head_count, DH)
        causal = key_pos[None, None, None, :] <= pos_group[:, :, None, None]
        own_block = (anchor_group == current)[:, None] & leading[None, :]
        allowed = (allow_group[:, :, :, None] != 0) & (
            jnp.logical_not(own_block)[:, None, :, None] | causal
        )
        part_list = []
        max_list = []
        total_list = []
        for head_lo in range(0, head_count, head_step):
            head_hi = head_lo + head_step
            scores = (
                jnp.einsum(
                    "gthd,auhd->ghtau",
                    q_group[:, :, head_lo:head_hi],
                    key_window[:, :, head_lo:head_hi],
                    preferred_element_type=jnp.float32,
                )
                * scaling
            )
            masked = jnp.where(allowed[:, None], scores, NEG_FILL)
            highest = jnp.max(masked, axis=(3, 4))
            weights = jnp.where(allowed[:, None], jnp.exp(masked - highest[..., None, None]), 0.0)
            total_list.append(jnp.sum(weights, axis=(3, 4)))
            max_list.append(highest)
            blended = jnp.einsum(
                "ghtau,auhd->gthd",
                weights.astype(jnp.bfloat16),
                value_window[:, :, head_lo:head_hi],
                preferred_element_type=jnp.float32,
            )
            part_list.append(blended.astype(jnp.bfloat16))
        partial_out = jnp.concatenate(part_list, axis=2).reshape(grouped, item_count, feature_width)
        class_max = jnp.transpose(jnp.concatenate(max_list, axis=1), (0, 2, 1))
        class_total = jnp.transpose(jnp.concatenate(total_list, axis=1), (0, 2, 1))
        return (partial_out, class_max, class_total)

    outer = sources // grouped
    reshaped = (
        query_rows.reshape(outer, grouped, item_count, feature_width),
        permitted.reshape(outer, grouped, item_count, span_count),
        position.reshape(outer, grouped, item_count),
        anchors.reshape(outer, grouped),
    )
    partial_out, class_max, class_total = lax.map(one_group, reshaped)
    return (
        partial_out.reshape(sources, item_count, feature_width).astype(jnp.float32),
        class_max.reshape(sources, item_count, head_count),
        class_total.reshape(sources, item_count, head_count),
    )


def merge_classes(partial_out, class_max, class_total):
    sources, block_len, feature_width = partial_out.shape
    head_count = class_max.shape[2]
    highest = jnp.max(class_max, axis=0)
    factor = jnp.exp(class_max - highest[None])
    denominator = jnp.sum(factor * class_total, axis=0)
    numerator = jnp.sum(
        factor[..., None] * partial_out.reshape(sources, block_len, head_count, DH), axis=0
    )
    return (
        (numerator / denominator[..., None]).reshape(block_len, feature_width).astype(jnp.bfloat16)
    )


def per_device(queries, keys, values, adjacency, counts):
    block_len, feature_width = queries.shape
    stripe_count = lax.axis_size("ka")
    current = lax.axis_index("ka")
    row_index = lax.axis_index("pb")
    stacked = jnp.stack([keys, values])
    window = [stacked]
    earlier = stacked
    for repeat in range(2):
        earlier = passed_along(earlier, "pb", 1)
        window.append(earlier)
    kv_window = jnp.stack(window, axis=1)
    span_count = len(window)
    lag_ids = jnp.arange(span_count, dtype=jnp.int32)
    slot_ids = jnp.arange(adjacency.shape[1], dtype=jnp.int32)
    positions = jnp.broadcast_to(
        jnp.arange(block_len, dtype=jnp.int32)[None, :], (stripe_count, block_len)
    )
    anchors = jnp.arange(stripe_count, dtype=jnp.int32)
    row_q, row_adj, row_cnt = (
        lax.all_gather(queries, "ka", axis=0, tiled=True),
        lax.all_gather(adjacency, "ka", axis=0, tiled=True),
        lax.all_gather(counts, "ka", axis=0, tiled=True),
    )
    wanted = (row_index - lag_ids) * stripe_count + current
    listed = (row_adj[:, None, :] == wanted[None, :, None]) & (
        slot_ids[None, None, :] < row_cnt[:, None, None]
    )
    present = jnp.any(listed, axis=2).astype(jnp.int32)
    permitted = jnp.broadcast_to(present[:, None, :], (stripe_count, block_len, span_count))
    partial_out, class_max, class_total = tile_partials(
        row_q.reshape(stripe_count, block_len, feature_width),
        permitted,
        positions,
        anchors,
        kv_window,
        current,
    )
    partial_out, class_max, class_total = (
        lax.all_to_all(partial_out, "ka", split_axis=0, concat_axis=0, tiled=True),
        lax.all_to_all(class_max, "ka", split_axis=0, concat_axis=0, tiled=True),
        lax.all_to_all(class_total, "ka", split_axis=0, concat_axis=0, tiled=True),
    )
    return merge_classes(partial_out, class_max, class_total)


def solution(mesh):
    in_specs = (
        P(("pb", "ka"), None),
        P(("pb", "ka"), None),
        P(("pb", "ka"), None),
        P(("pb", "ka"), None),
        P(("pb", "ka")),
    )
    out_specs = P(("pb", "ka"), None)
    return jax.shard_map(
        per_device, mesh=mesh, in_specs=in_specs, out_specs=out_specs, check_vma=False
    )
```

profile of v0, /device:TPU:30, one launch (start us, length us, event | category | flops | bytes accessed | tf_op | source)
XLA Modules:
  0.0 505.4 jit_solution(13718441947726245500)
XLA Ops:
  7.3 1.2 copy.75
  8.5 1.2 copy.76
  9.8 4.6 collective-permute-start
  14.4 16.8 %collective-permute-done = bf16[2,128,1536]{1,2,0:T(8,128)(2,1)S(1)} collective-permute-done((bf16[2,128,1536]{1,2,0:T(8,128)(2,1)S(1)}, bf16[2,128,1536]{1,2,0:T(8,128)(2,1)S(1)}, u32[]{:S(2)}, u32[]{:S(2)}) %collective-permute-start) | collective-permute-done | bytes 786464 | tf_op jit(solution)/shard_map/ppermute | solution.py:14
  31.2 7.7 %collective-permute-start.1 = (bf16[2,128,1536]{1,2,0:T(8,128)(2,1)S(1)}, bf16[2,128,1536]{1,2,0:T(8,128)(2,1)S(1)}, u32[]{:S(2)}, u32[]{:S(2)}) collective-permute-start(bf16[2,128,1536]{1,2,0:T(8,128)(2,1)S(1)} %collective-permute-done), channel_id=1, source_target_pairs={{0,16},{16,32},{32,48},{48,64},{64,80},{80,96},{96,112},{112,128},... | collective-permute-start | bytes 2359304 | tf_op jit(solution)/shard_map/ppermute | solution.py:14
  39.6 1.3 dynamic-slice
  41.5 20.1 %all-reduce = s32[16]{0:T(128)S(1)} all-reduce(s32[16]{0:T(128)S(1)} %dynamic-update-slice), channel_id=1, replica_groups=mesh['pb'=32,'ka'=16] {'ka'}, use_global_device_ids=true, to_apply=%add | all-reduce | flops 16 | bytes 128
  61.6 15.1 %all-gather = s32[16,1,24]{2,1,0:T(1,128)S(1)} all-gather(s32[1,1,24]{2,1,0:T(1,128)S(1)} %bitcast.255), channel_id=1, replica_groups=mesh['pb'=32,'ka'=16] {'ka'}, dimensions={0}, use_global_device_ids=true | all-gather | bytes 1632 | tf_op jit(solution)/shard_map/all_gather | solution.py:119
  77.6 1.4 copy.80
  80.2 105.2 %while.15 = (s32[]{:T(128)}, bf16[4,4,128,1536]{2,3,1,0:T(8,128)(2,1)}, f32[4,4,128,12]{2,1,0,3:T(4,128)S(1)}, f32[4,4,128,12]{2,1,0,3:T(4,128)}, s32[4,4,128,3]...) while((s32[]{:T(128)}, ...), condition=%wide.region_8.9_spmd.clone, body=%wide.region_1.8_spmd.clone.sunk | while | flops 1241462272 | bytes 78790904 | solution.py:76
  80.6 1.5 constant_dynamic-slice_fusion.3
  83.0 1.1 fusion.116
  85.2 1.7 fusion.117
  86.9 2.0 copy.120
  88.9 4.0 bitcast_reduce_fusion.4
  92.9 2.0 copy.121
  95.0 4.6 fusion.118
  105.2 1.3 constant_dynamic-update-slice_fusion.2
  106.9 1.5 constant_dynamic-slice_fusion.3
  111.5 1.7 fusion.117
  113.2 2.0 copy.120
  115.2 4.0 bitcast_reduce_fusion.4
  119.2 2.0 copy.121
  121.3 4.6 fusion.118
  131.5 1.3 constant_dynamic-update-slice_fusion.2
  133.1 1.5 constant_dynamic-slice_fusion.3
  135.6 1.1 fusion.116
  137.7 1.7 fusion.117
  139.5 2.0 copy.120
  141.5 4.0 bitcast_reduce_fusion.4
  145.5 2.0 copy.121
  147.5 4.6 fusion.118
  157.8 1.3 constant_dynamic-update-slice_fusion.2
  159.4 1.5 constant_dynamic-slice_fusion.3
  164.0 1.7 fusion.117
  165.7 2.0 copy.120
  167.8 4.0 bitcast_reduce_fusion.4
  171.8 2.0 copy.121
  173.8 4.7 fusion.118
  184.1 1.3 constant_dynamic-update-slice_fusion.2
  186.0 3.9 all-to-all-start
  190.0 1.6 copy.85
  191.6 7.1 %all-to-all-done = f32[16,128,12]{1,2,0:T(8,128)S(1)} async-done(((f32[16,128,12]{1,2,0:T(8,128)}), f32[16,128,12]{1,2,0:T(8,128)S(1)}, u32[]{:S(2)}, u32[]{:S(2)}) %all-to-all-start) | async-done | bytes 98336 | tf_op jit(solution)/shard_map/all_to_all | solution.py:138
  198.6 3.7 all-to-all-start.2
  202.3 8.6 %bitcast_convert_fusion = f32[16,128,1536]{1,2,0:T(8,128)} fusion(bf16[4,4,128,1536]{2,3,1,0:T(8,128)(2,1)} %get-tuple-element.75), kind=kLoop, calls=%fused_computation.86 | loop fusion | flops 3145728 | bytes 18874368 | tf_op jit(solution)/shard_map/convert_element_type | solution.py:78
  211.0 7.0 %all-to-all-start.1 = ((f32[16,128,1536]{1,2,0:T(8,128)}), f32[16,128,1536]{1,2,0:T(8,128)}, u32[]{:S(2)}, u32[]{:S(2)}) async-start(f32[16,128,1536]{1,2,0:T(8,128)} %bitcast_convert_fusion), calls=%async_computation.1 | async-start | bytes 25165824 | tf_op jit(solution)/shard_map/all_to_all | solution.py:137
  218.0 274.0 %all-to-all-done.1 = f32[16,128,1536]{1,2,0:T(8,128)} async-done(((f32[16,128,1536]{1,2,0:T(8,128)}), f32[16,128,1536]{1,2,0:T(8,128)}, u32[]{:S(2)}, u32[]{:S(2)}) %all-to-all-start.1) | async-done | bytes 12582944 | tf_op jit(solution)/shard_map/all_to_all | solution.py:137
  492.0 5.6 %fusion.85 = f32[128,1536]{0,1:T(8,128)S(1)} fusion(f32[16,128,1536]{1,2,0:T(8,128)} %all-to-all-done.1, f32[16,128,12]{1,2,0:T(8,128)S(1)} %get-tuple-element.174), kind=kLoop, calls=%fused_computation.85 | loop fusion | flops 6094848 | bytes 13467648 | tf_op jit(solution)/shard_map/reduce_sum | solution.py:90
  (111 shorter events, 38.8 us)
Async XLA Ops:
  6.5 55.1 %copy-start.2 = (s32[1,24]{1,0:T(1,128)S(1)}, s32[1,24]{1,0:T(1,128)}, u32[]{:S(2)}) copy-start(s32[1,24]{1,0:T(1,128)} %param.10) | copy-start | bytes 292
  6.5 73.6 %all-gather.3.cloned.1.call-start = ((), (), s32[]{:S(2)}) async-start(), calls=%async_computation.3 | async-start | bytes 6684672 | tf_op jit(solution)/shard_map/all_gather | solution.py:118
  9.8 21.4 %collective-permute-start = (bf16[2,128,1536]{1,2,0:T(8,128)(2,1)S(1)}, bf16[2,128,1536]{1,2,0:T(8,128)(2,1)S(1)}, u32[]{:S(2)}, u32[]{:S(2)}) collective-permute-start(bf16[2,128,1536]{1,2,0:T(8,128)(2,1)S(1)} %get-tuple-element.185), channel_id=1, source_target_pairs={{0,16},{16,32},{32,48},{48,64},{64,80},{80,96},{96,112},{112,128},... | collective-permute-start | bytes 2359304 | tf_op jit(solution)/shard_map/ppermute | solution.py:14
  31.2 46.0 %collective-permute-start.1 = (bf16[2,128,1536]{1,2,0:T(8,128)(2,1)S(1)}, bf16[2,128,1536]{1,2,0:T(8,128)(2,1)S(1)}, u32[]{:S(2)}, u32[]{:S(2)}) collective-permute-start(bf16[2,128,1536]{1,2,0:T(8,128)(2,1)S(1)} %collective-permute-done), channel_id=1, source_target_pairs={{0,16},{16,32},{32,48},{48,64},{64,80},{80,96},{96,112},{112,128},... | collective-permute-start | bytes 2359304 | tf_op jit(solution)/shard_map/ppermute | solution.py:14
  95.0 6.1 %copy-start.1 = (bf16[3,128,12,128]{1,3,0,2:T(8,128)(2,1)S(1)}, bf16[3,128,12,128]{1,3,0,2:T(8,128)(2,1)}, u32[]{:S(2)}) copy-start(bf16[3,128,12,128]{1,3,0,2:T(8,128)(2,1)} %get-tuple-element.311) | copy-start | bytes 3538948 | tf_op jit(solution)/shard_map/while
  99.6 1.9 copy-start
  121.3 6.1 %copy-start.1 = (bf16[3,128,12,128]{1,3,0,2:T(8,128)(2,1)S(1)}, bf16[3,128,12,128]{1,3,0,2:T(8,128)(2,1)}, u32[]{:S(2)}) copy-start(bf16[3,128,12,128]{1,3,0,2:T(8,128)(2,1)} %get-tuple-element.311) | copy-start | bytes 3538948 | tf_op jit(solution)/shard_map/while
  125.9 1.9 copy-start
  147.5 6.1 %copy-start.1 = (bf16[3,128,12,128]{1,3,0,2:T(8,128)(2,1)S(1)}, bf16[3,128,12,128]{1,3,0,2:T(8,128)(2,1)}, u32[]{:S(2)}) copy-start(bf16[3,128,12,128]{1,3,0,2:T(8,128)(2,1)} %get-tuple-element.311) | copy-start | bytes 3538948 | tf_op jit(solution)/shard_map/while
  152.2 1.9 copy-start
  173.8 6.1 %copy-start.1 = (bf16[3,128,12,128]{1,3,0,2:T(8,128)(2,1)S(1)}, bf16[3,128,12,128]{1,3,0,2:T(8,128)(2,1)}, u32[]{:S(2)}) copy-start(bf16[3,128,12,128]{1,3,0,2:T(8,128)(2,1)} %get-tuple-element.311) | copy-start | bytes 3538948 | tf_op jit(solution)/shard_map/while
  178.5 1.9 copy-start
  186.0 12.6 %all-to-all-start = ((f32[16,128,12]{1,2,0:T(8,128)}), f32[16,128,12]{1,2,0:T(8,128)S(1)}, u32[]{:S(2)}, u32[]{:S(2)}) async-start(f32[16,128,12]{1,2,0:T(8,128)} %copy.83), calls=%async_computation | async-start | bytes 262144 | tf_op jit(solution)/shard_map/all_to_all | solution.py:138
  198.6 12.3 %all-to-all-start.2 = ((f32[16,128,12]{1,2,0:T(8,128)}), f32[16,128,12]{1,2,0:T(8,128)S(1)}, u32[]{:S(2)}, u32[]{:S(2)}) async-start(f32[16,128,12]{1,2,0:T(8,128)} %copy.85), calls=%async_computation.2 | async-start | bytes 262144 | tf_op jit(solution)/shard_map/all_to_all | solution.py:139
  211.0 281.0 %all-to-all-start.1 = ((f32[16,128,1536]{1,2,0:T(8,128)}), f32[16,128,1536]{1,2,0:T(8,128)}, u32[]{:S(2)}, u32[]{:S(2)}) async-start(f32[16,128,1536]{1,2,0:T(8,128)} %bitcast_convert_fusion), calls=%async_computation.1 | async-start | bytes 25165824 | tf_op jit(solution)/shard_map/all_to_all | solution.py:137
Sparse Core Ops, SparseCore 0:
  9.5 53.8 all-gather.2
where the time goes:
time: 507 us; the launch traced here: 505 us
  waiting for transfers between devices  299 us (59%)
  matrix products  54.7 us (11%)
  local copies, waits for them, and re-layouts  52.6 us (10%)
  blocking collectives  35.2 us (7%)
  starting transfers between devices  26.9 us (5%)
  other arithmetic  22.8 us (4%)
  between operations  14.2 us (3%)
    all_to_all x1, waiting for transfers between devices, per_device(): lax.all_to_all(partial_out, 'ka', split_axis=0, concat_axis=0, tiled=True)  274 us
    dot_general x12, matrix products, one_group(): jnp.einsum('gthd,auhd->ghtau', q_group[:, :, head_lo:head_hi], key_window...  41.4 us
    while x28, local copies, waits for them, and re-layouts  22.3 us
    unnamed x1, blocking collectives  20.1 us
    ppermute x2, waiting for transfers between devices, passed_along(): return lax.ppermute(block, axis, route)  16.8 us
    all_gather x1, blocking collectives, per_device(): lax.all_gather(adjacency, 'ka', axis=0, tiled=True)  15.1 us
    dot_general x12, matrix products, one_group(): jnp.einsum('ghtau,auhd->gthd', weights.astype(jnp.bfloat16), value_window...  13.3 us
    ppermute x2, starting transfers between devices, passed_along(): return lax.ppermute(block, axis, route)  12.3 us
  transfers between devices with their start and end apart: 6, of which 3 were waited for; matrix products, arithmetic and copies ran while one was open for 4% of the time, Pallas kernels for 0%

commit v1 on v0

--- a/solution.py
+++ b/solution.py
@@ -114,9 +114,26 @@
         jnp.arange(block_len, dtype=jnp.int32)[None, :], (stripe_count, block_len)
     )
     anchors = jnp.arange(stripe_count, dtype=jnp.int32)
+
+    def _switch_files(x_part):
+        n_chips = lax.axis_size("ka")
+        heap = tuple(((num, (num + 1) % n_chips) for num in range(n_chips)))
+        nodes = tuple(((num, (num - 1) % n_chips) for num in range(n_chips)))
+        x_next, small = ([x_part], [x_part])
+        for _ in range(n_chips // 2):
+            x_next.append(lax.ppermute(x_next[-1], perm=heap, axis_name="ka"))
+        rr = 0
+        while rr < (n_chips - 1) // 2:
+            val = lax.ppermute(small[-1], "ka", perm=nodes)
+            small.append(val)
+            rr += 1
+        arr_out = jnp.concatenate([*x_next[::-1], *small[1:]], axis=0)
+        e_next = jnp.roll(arr_out, (lax.axis_index("ka") - n_chips // 2) * x_part.shape[0], axis=0)
+        return e_next
+
     row_q, row_adj, row_cnt = (
         lax.all_gather(queries, "ka", axis=0, tiled=True),
-        lax.all_gather(adjacency, "ka", axis=0, tiled=True),
+        _switch_files(adjacency),
         lax.all_gather(counts, "ka", axis=0, tiled=True),
     )
     wanted = (row_index - lag_ids) * stripe_count + current

time: 507 us -> 523 us (1.032)
  starting transfers between devices: 26.9 us -> 51.4 us
  blocking collectives: 35.2 us -> 14.5 us
  waiting for transfers between devices: 299 us -> 310 us
    ppermute x0 -> x15, starting transfers between devices: none -> 24.9 us  [the longest x7 24.8 us: _switch_files(): val = lax.ppermute(small[-1], 'ka', perm=nodes)]
    all_gather x1 -> x0, blocking collectives: 15.1 us -> none  [per_device(): lax.all_gather(adjacency, 'ka', axis=0, tiled=True)]
    ppermute x0 -> x15, waiting for transfers between devices: none -> 11.9 us  [the longest x8 11.6 us: _switch_files(): x_next.append(lax.ppermute(x_next[-1], perm=heap, axis_name='ka'))]
    unnamed x1, blocking collectives: 20.1 us -> 14.5 us
  transfers between devices with their start and end apart: 6 -> 21, of which waited for: 3 -> 10; matrix products, arithmetic and copies ran while one was open for 4% -> 3% of each run, Pallas kernels for 0% -> 0%
where the time goes in v1:
time: 523 us; the launch traced here: 521 us
  waiting for transfers between devices  310 us (59%)
  matrix products  54.7 us (10%)
  local copies, waits for them, and re-layouts  52.8 us (10%)
  starting transfers between devices  51.4 us (10%)
  other arithmetic  22.7 us (4%)
  blocking collectives  14.5 us (3%)
  between operations  14.2 us (3%)
    all_to_all x1, waiting for transfers between devices, per_device(): lax.all_to_all(partial_out, 'ka', split_axis=0, concat_axis=0, tiled=True)  274 us
    dot_general x12, matrix products, one_group(): jnp.einsum('gthd,auhd->ghtau', q_group[:, :, head_lo:head_hi], key_window...  41.4 us
    ppermute x7, starting transfers between devices, _switch_files(): val = lax.ppermute(small[-1], 'ka', perm=nodes)  24.8 us
    while x28, local copies, waits for them, and re-layouts  22.3 us
    ppermute x2, waiting for transfers between devices, passed_along(): return lax.ppermute(block, axis, route)  16.8 us
    unnamed x1, blocking collectives  14.5 us
    dot_general x12, matrix products, one_group(): jnp.einsum('ghtau,auhd->gthd', weights.astype(jnp.bfloat16), value_window...  13.3 us
    ppermute x2, starting transfers between devices, passed_along(): return lax.ppermute(block, axis, route)  12.3 us
  transfers between devices with their start and end apart: 21, of which 10 were waited for; matrix products, arithmetic and copies ran while one was open for 3% of the time, Pallas kernels for 0%

profile of v1, /device:TPU:30, one launch (start us, length us, event | category | flops | bytes accessed | tf_op | source)
XLA Modules:
  0.0 521.1 jit_solution(479312939483987374)
XLA Ops:
  9.8 4.6 collective-permute-start.15
  14.4 16.8 %collective-permute-done.15 = bf16[2,128,1536]{1,2,0:T(8,128)(2,1)S(1)} collective-permute-done((bf16[2,128,1536]{1,2,0:T(8,128)(2,1)S(1)}, bf16[2,128,1536]{1,2,0:T(8,128)(2,1)S(1)}, u32[]{:S(2)}, u32[]{:S(2)}) %collective-permute-start.15) | collective-permute-done | bytes 786464 | tf_op jit(solution)/shard_map/ppermute | solution.py:14
  31.2 7.7 %collective-permute-start.16 = (bf16[2,128,1536]{1,2,0:T(8,128)(2,1)S(1)}, bf16[2,128,1536]{1,2,0:T(8,128)(2,1)S(1)}, u32[]{:S(2)}, u32[]{:S(2)}) collective-permute-start(bf16[2,128,1536]{1,2,0:T(8,128)(2,1)S(1)} %collective-permute-done.15), channel_id=1, source_target_pairs={{0,16},{16,32},{32,48},{48,64},{64,80},{80,96},{96,112},{112,128},... | collective-permute-start | bytes 2359304 | tf_op jit(solution)/shard_map/ppermute | solution.py:14
  39.0 7.4 %collective-permute-start.8 = (s32[1,24]{1,0:T(1,128)S(1)}, s32[1,24]{1,0:T(1,128)S(1)}, u32[]{:S(2)}, u32[]{:S(2)}) collective-permute-start(s32[1,24]{1,0:T(1,128)S(1)} %copy-done.2), channel_id=1, source_target_pairs={{0,15},{1,0},{2,1},{3,2},{4,3},{5,4},{6,5},{7,6},{8,7},{9,8},{10,9... | collective-permute-start | bytes 296 | tf_op jit(solution)/shard_map/ppermute | solution.py:127
  48.9 14.5 %all-reduce = s32[16]{0:T(128)S(1)} all-reduce(s32[16]{0:T(128)S(1)} %dynamic-update-slice), channel_id=1, replica_groups=mesh['pb'=32,'ka'=16] {'ka'}, use_global_device_ids=true, to_apply=%add | all-reduce | flops 16 | bytes 128
  63.5 2.9 collective-permute-start.9
  67.7 2.9 collective-permute-start.10
  71.9 2.9 collective-permute-start.11
  76.1 2.9 collective-permute-start.12
  80.3 2.9 collective-permute-start.13
  84.6 2.9 collective-permute-start.14
  88.8 4.2 collective-permute-done.7
  93.8 1.4 copy.80
  96.4 105.1 %while.15 = (s32[]{:T(128)}, bf16[4,4,128,1536]{2,3,1,0:T(8,128)(2,1)}, f32[4,4,128,12]{2,1,0,3:T(4,128)S(1)}, f32[4,4,128,12]{2,1,0,3:T(4,128)}, s32[4,4,128,3]...) while((s32[]{:T(128)}, ...), condition=%wide.region_8.9_spmd.clone, body=%wide.region_1.8_spmd.clone.sunk | while | flops 1241462272 | bytes 78790904 | solution.py:76
  96.8 1.5 constant_dynamic-slice_fusion.4
  101.3 1.7 fusion.117
  103.1 2.0 copy.120
  105.1 4.0 bitcast_reduce_fusion.4
  109.1 2.0 copy.121
  111.1 4.6 fusion.118
  121.4 1.3 constant_dynamic-update-slice_fusion.2
  123.1 1.5 constant_dynamic-slice_fusion.4
  127.6 1.7 fusion.117
  129.4 2.0 copy.120
  131.4 4.0 bitcast_reduce_fusion.4
  135.4 2.0 copy.121
  137.5 4.6 fusion.118
  149.3 1.5 constant_dynamic-slice_fusion.4
  153.9 1.7 fusion.117
  155.6 2.0 copy.120
  157.7 4.0 bitcast_reduce_fusion.4
  161.7 2.0 copy.121
  163.7 4.6 fusion.118
  175.6 1.5 constant_dynamic-slice_fusion.4
  180.2 1.7 fusion.117
  181.9 2.0 copy.120
  183.9 4.0 bitcast_reduce_fusion.4
  187.9 2.0 copy.121
  190.0 4.6 fusion.118
  200.2 1.3 constant_dynamic-update-slice_fusion.2
  202.2 3.5 all-to-all-start
  205.7 1.6 copy.85
  207.3 7.0 %all-to-all-done = f32[16,128,12]{1,2,0:T(8,128)S(1)} async-done(((f32[16,128,12]{1,2,0:T(8,128)}), f32[16,128,12]{1,2,0:T(8,128)S(1)}, u32[]{:S(2)}, u32[]{:S(2)}) %all-to-all-start) | async-done | bytes 98336 | tf_op jit(solution)/shard_map/all_to_all | solution.py:155
  214.3 3.7 all-to-all-start.2
  218.0 8.6 %bitcast_convert_fusion = f32[16,128,1536]{1,2,0:T(8,128)} fusion(bf16[4,4,128,1536]{2,3,1,0:T(8,128)(2,1)} %get-tuple-element.75), kind=kLoop, calls=%fused_computation.86 | loop fusion | flops 3145728 | bytes 18874368 | tf_op jit(solution)/shard_map/convert_element_type | solution.py:78
  226.6 7.0 %all-to-all-start.1 = ((f32[16,128,1536]{1,2,0:T(8,128)}), f32[16,128,1536]{1,2,0:T(8,128)}, u32[]{:S(2)}, u32[]{:S(2)}) async-start(f32[16,128,1536]{1,2,0:T(8,128)} %bitcast_convert_fusion), calls=%async_computation.1 | async-start | bytes 25165824 | tf_op jit(solution)/shard_map/all_to_all | solution.py:154
  233.7 274.0 %all-to-all-done.1 = f32[16,128,1536]{1,2,0:T(8,128)} async-done(((f32[16,128,1536]{1,2,0:T(8,128)}), f32[16,128,1536]{1,2,0:T(8,128)}, u32[]{:S(2)}, u32[]{:S(2)}) %all-to-all-start.1) | async-done | bytes 12582944 | tf_op jit(solution)/shard_map/all_to_all | solution.py:154
  507.7 5.6 %fusion.85 = f32[128,1536]{0,1:T(8,128)S(1)} fusion(f32[16,128,1536]{1,2,0:T(8,128)} %all-to-all-done.1, f32[16,128,12]{1,2,0:T(8,128)S(1)} %get-tuple-element.174), kind=kLoop, calls=%fused_computation.85 | loop fusion | flops 6094848 | bytes 13467648 | tf_op jit(solution)/shard_map/reduce_sum | solution.py:90
  (142 shorter events, 55.1 us)
Async XLA Ops:
  6.5 32.4 %copy-start.2 = (s32[1,24]{1,0:T(1,128)S(1)}, s32[1,24]{1,0:T(1,128)}, u32[]{:S(2)}) copy-start(s32[1,24]{1,0:T(1,128)} %param.10) | copy-start | bytes 292
  6.5 89.8 %all-gather.2.cloned.1.call-start = ((), (), s32[]{:S(2)}) async-start(), calls=%async_computation.3 | async-start | bytes 6684672 | tf_op jit(solution)/shard_map/all_gather | solution.py:135
  9.8 21.4 %collective-permute-start.15 = (bf16[2,128,1536]{1,2,0:T(8,128)(2,1)S(1)}, bf16[2,128,1536]{1,2,0:T(8,128)(2,1)S(1)}, u32[]{:S(2)}, u32[]{:S(2)}) collective-permute-start(bf16[2,128,1536]{1,2,0:T(8,128)(2,1)S(1)} %get-tuple-element.185), channel_id=1, source_target_pairs={{0,16},{16,32},{32,48},{48,64},{64,80},{80,96},{96,112},{112,128},... | collective-permute-start | bytes 2359304 | tf_op jit(solution)/shard_map/ppermute | solution.py:14
  31.2 62.1 %collective-permute-start.16 = (bf16[2,128,1536]{1,2,0:T(8,128)(2,1)S(1)}, bf16[2,128,1536]{1,2,0:T(8,128)(2,1)S(1)}, u32[]{:S(2)}, u32[]{:S(2)}) collective-permute-start(bf16[2,128,1536]{1,2,0:T(8,128)(2,1)S(1)} %collective-permute-done.15), channel_id=1, source_target_pairs={{0,16},{16,32},{32,48},{48,64},{64,80},{80,96},{96,112},{112,128},... | collective-permute-start | bytes 2359304 | tf_op jit(solution)/shard_map/ppermute | solution.py:14
  38.9 24.5 %collective-permute-start = (s32[1,24]{1,0:T(1,128)S(1)}, s32[1,24]{1,0:T(1,128)S(1)}, u32[]{:S(2)}, u32[]{:S(2)}) collective-permute-start(s32[1,24]{1,0:T(1,128)S(1)} %copy-done.2), channel_id=1, source_target_pairs={{0,1},{1,2},{2,3},{3,4},{4,5},{5,6},{6,7},{7,8},{8,9},{9,10},{10,1... | collective-permute-start | bytes 296 | tf_op jit(solution)/shard_map/ppermute | solution.py:124
  39.0 24.5 %collective-permute-start.8 = (s32[1,24]{1,0:T(1,128)S(1)}, s32[1,24]{1,0:T(1,128)S(1)}, u32[]{:S(2)}, u32[]{:S(2)}) collective-permute-start(s32[1,24]{1,0:T(1,128)S(1)} %copy-done.2), channel_id=1, source_target_pairs={{0,15},{1,0},{2,1},{3,2},{4,3},{5,4},{6,5},{7,6},{8,7},{9,8},{10,9... | collective-permute-start | bytes 296 | tf_op jit(solution)/shard_map/ppermute | solution.py:127
  63.5 4.2 collective-permute-start.1
  63.5 4.2 collective-permute-start.9
  67.7 4.2 collective-permute-start.2
  67.7 4.2 collective-permute-start.10
  71.9 4.2 collective-permute-start.3
  71.9 4.2 collective-permute-start.11
  76.1 4.2 collective-permute-start.4
  76.1 4.2 collective-permute-start.12
  80.3 4.2 collective-permute-start.5
  80.3 4.2 collective-permute-start.13
  84.5 4.2 collective-permute-start.6
  84.6 4.2 collective-permute-start.14
  88.7 4.2 collective-permute-start.7
  111.1 6.1 %copy-start.1 = (bf16[3,128,12,128]{1,3,0,2:T(8,128)(2,1)S(1)}, bf16[3,128,12,128]{1,3,0,2:T(8,128)(2,1)}, u32[]{:S(2)}) copy-start(bf16[3,128,12,128]{1,3,0,2:T(8,128)(2,1)} %get-tuple-element.311) | copy-start | bytes 3538948 | tf_op jit(solution)/shard_map/while
  115.8 1.9 copy-start
  137.4 6.1 %copy-start.1 = (bf16[3,128,12,128]{1,3,0,2:T(8,128)(2,1)S(1)}, bf16[3,128,12,128]{1,3,0,2:T(8,128)(2,1)}, u32[]{:S(2)}) copy-start(bf16[3,128,12,128]{1,3,0,2:T(8,128)(2,1)} %get-tuple-element.311) | copy-start | bytes 3538948 | tf_op jit(solution)/shard_map/while
  142.1 1.9 copy-start
  163.7 6.1 %copy-start.1 = (bf16[3,128,12,128]{1,3,0,2:T(8,128)(2,1)S(1)}, bf16[3,128,12,128]{1,3,0,2:T(8,128)(2,1)}, u32[]{:S(2)}) copy-start(bf16[3,128,12,128]{1,3,0,2:T(8,128)(2,1)} %get-tuple-element.311) | copy-start | bytes 3538948 | tf_op jit(solution)/shard_map/while
  168.4 1.9 copy-start
  190.0 6.1 %copy-start.1 = (bf16[3,128,12,128]{1,3,0,2:T(8,128)(2,1)S(1)}, bf16[3,128,12,128]{1,3,0,2:T(8,128)(2,1)}, u32[]{:S(2)}) copy-start(bf16[3,128,12,128]{1,3,0,2:T(8,128)(2,1)} %get-tuple-element.311) | copy-start | bytes 3538948 | tf_op jit(solution)/shard_map/while
  194.6 1.9 copy-start
  202.2 12.1 %all-to-all-start = ((f32[16,128,12]{1,2,0:T(8,128)}), f32[16,128,12]{1,2,0:T(8,128)S(1)}, u32[]{:S(2)}, u32[]{:S(2)}) async-start(f32[16,128,12]{1,2,0:T(8,128)} %copy.83), calls=%async_computation | async-start | bytes 262144 | tf_op jit(solution)/shard_map/all_to_all | solution.py:155
  214.3 12.3 %all-to-all-start.2 = ((f32[16,128,12]{1,2,0:T(8,128)}), f32[16,128,12]{1,2,0:T(8,128)S(1)}, u32[]{:S(2)}, u32[]{:S(2)}) async-start(f32[16,128,12]{1,2,0:T(8,128)} %copy.85), calls=%async_computation.2 | async-start | bytes 262144 | tf_op jit(solution)/shard_map/all_to_all | solution.py:156
  226.6 281.0 %all-to-all-start.1 = ((f32[16,128,1536]{1,2,0:T(8,128)}), f32[16,128,1536]{1,2,0:T(8,128)}, u32[]{:S(2)}, u32[]{:S(2)}) async-start(f32[16,128,1536]{1,2,0:T(8,128)} %bitcast_convert_fusion), calls=%async_computation.1 | async-start | bytes 25165824 | tf_op jit(solution)/shard_map/all_to_all | solution.py:154
Sparse Core Ops, SparseCore 0:
  9.5 53.7 all-gather.1
